TPU v7x, 32 devices: a whole 2x2x4 slice. The times are simulated.
32 devices in a mesh: seq: 4 (over z), ch: 8 (over y, x, core).
Axes of the slice: x: 2, y: 2, z: 4, core: 2. Of those that a mesh axis runs over, the one named last changes fastest.
Arguments:
- inputs: bfloat16 [1024, 8192], P('seq', 'ch'), may hold values from -6 to 6
- w_in: bfloat16 [3, 8192, 8192], P(None, 'seq', 'ch'), may hold values from -0.0625 to 0.0625
- short_filter: float32 [3, 3, 8192], P(None, None, 'ch'), may hold values from -3 to 3
- rates: float32 [16, 8192], P(None, 'ch'), may hold values from 9.765625e-05 to 0.05
- residues: float32 [16, 8192], P(None, 'ch'), may hold values from -3 to 3
- skip: float32 [8192], P('ch'), may hold values from -3 to 3
Outputs:
- gated: bfloat16 [1024, 8192], P('seq', 'ch')
All inputs are finite; a program needn't handle non-finite values.
Results may differ from a plain program's by a relative error of at most 0.0065.
Values may be sent and summed in bfloat16 or wider, within the bound.
No kernel may reach another device: no remote copies, remote signals or barrier semaphores. Data moves between devices by JAX's collectives and lax.ppermute only.
A program may use at most 128 MiB of HBM per device.

v0:
```python
import jax
import jax.numpy as jnp
from jax import lax
from jax.sharding import PartitionSpec as P

TAPS = 3


def passed_along(block, axis, distance):
    devices = range(lax.axis_size(axis))
    route = [(i - distance, i) for i in devices if i - distance in devices]
    return lax.ppermute(block, axis, route)


def carried_in(part, axis, combine, identity):
    place = lax.axis_index(axis)
    gathered = jax.tree.map(lambda a: lax.all_gather(a, axis), part)
    state = jax.tree.map(lambda a, e: jnp.zeros_like(a) + jnp.asarray(e, a.dtype), part, identity)

    def one(hop, state):
        return combine(
            state, jax.tree.map(lambda a: lax.dynamic_index_in_dim(a, hop, 0, False), gathered)
        )

    return lax.fori_loop(0, place, one, state)


def combine(earlier, later):
    return (earlier[0] * later[0], earlier[1] * later[0] + later[1])


def per_device(inputs, w_in, short_filter, rates, residues, skip):
    tok_rows = inputs.shape[0]
    width = w_in.shape[2]
    modes = rates.shape[0]
    features = lax.all_gather(inputs, "ch", axis=1, tiled=True)
    proj = jnp.einsum(
        "td,kdc->ktc",
        features,
        lax.all_gather(w_in, "seq", axis=1, tiled=True),
        preferred_element_type=jnp.float32,
    ).astype(jnp.bfloat16)
    prior = passed_along(proj[:, tok_rows - (TAPS - 1) :, :], "seq", 1)
    padded = jnp.concatenate([prior, proj], axis=1).astype(jnp.float32)
    mixed = jnp.zeros((3, tok_rows, width), jnp.float32)
    for j in range(TAPS):
        mixed = (
            mixed
            + short_filter[:, j, None, :] * padded[:, TAPS - 1 - j : TAPS - 1 - j + tok_rows, :]
        )
    query, key, value = (mixed[0], mixed[1], mixed[2])
    drive = key * value
    position = jnp.arange(tok_rows, dtype=jnp.float32)
    scaled = residues * jnp.sqrt(1.0 - jnp.exp(-2.0 * rates))
    end_powers = jnp.exp(-rates[None, :, :] * (tok_rows - 1.0 - position)[:, None, None])
    end_state = jnp.sum(end_powers * drive[:, None, :], axis=0)
    block_decay = jnp.exp(-rates * tok_rows)
    identity = (jnp.ones_like(block_decay), jnp.zeros_like(end_state))
    entering = carried_in((block_decay, end_state), "seq", combine, identity)[1]
    start_powers = jnp.exp(-rates[None, :, :] * (position + 1.0)[:, None, None])
    cross = jnp.sum(start_powers * (scaled * entering)[None, :, :], axis=1)
    center = (tok_rows - 1.0) / 2.0
    offset = (position - center)[:, None, None]
    rising = jnp.exp(rates[None, :, :] * offset) * drive[:, None, :]
    offsets = jnp.arange(tok_rows, dtype=jnp.int32)
    lower = (offsets[:, None] >= offsets[None, :]).astype(jnp.float32)
    prefix = jnp.dot(
        lower, rising.reshape(tok_rows, modes * width), precision=lax.Precision.HIGHEST
    )
    prefix = prefix.reshape(tok_rows, modes, width)
    falling = jnp.exp(-rates[None, :, :] * offset) * scaled[None, :, :]
    local = jnp.sum(falling * prefix, axis=1)
    return (query * (local + cross + skip[None, :] * drive)).astype(jnp.bfloat16)


def solution(mesh):
    in_specs = (
        P("seq", "ch"),
        P(None, "seq", "ch"),
        P(None, None, "ch"),
        P(None, "ch"),
        P(None, "ch"),
        P("ch"),
    )
    out_specs = P("seq", "ch")
    return jax.shard_map(
        per_device, mesh=mesh, in_specs=in_specs, out_specs=out_specs, check_vma=False
    )
```

profile of v0, /device:TPU:0, one launch (start us, length us, event | category | flops | bytes accessed | tf_op | source)
XLA Modules:
  0.0 979.4 jit_solution(17450163939474768816)
XLA Ops:
  6.5 0.7 all-gather.7.cloned.1.call-update
  7.3 0.0 all-gather.5.cloned.1.call-start
  7.3 0.7 all-gather.5.cloned.1.call-update
  8.0 0.9 fusion.17
  9.0 1.5 fusion.16
  10.5 38.1 %all-gather.7.cloned.1.call-done = bf16[256,8192]{1,0:T(8,128)(2,1)} async-done(((bf16[256,1024]{1,0:T(8,128)(2,1)}), bf16[256,8192]{1,0:T(8,128)(2,1)}) %all-gather.7.cloned.1.call-update) | async-done | bytes 4194320 | tf_op jit(solution)/shard_map/all_gather | solution.py:36
  48.6 837.6 %all-gather.5.cloned.1.call-done = bf16[3,8192,1024]{2,1,0:T(8,128)(2,1)} async-done(((bf16[3,2048,1024]{2,1,0:T(8,128)(2,1)}), bf16[3,8192,1024]{2,1,0:T(8,128)(2,1)}) %all-gather.5.cloned.1.call-update) | async-done | bytes 50331664 | tf_op jit(solution)/shard_map/all_gather | solution.py:40
  886.2 21.8 %fusion.7 = bf16[3,256,1024]{2,1,0:T(8,128)(2,1)S(1)} fusion(bf16[3,8192,1024]{2,1,0:T(8,128)(2,1)} %all-gather.5.cloned.1.call-done, bf16[256,8192]{1,0:T(8,128)(2,1)} %all-gather.7.cloned.1.call-done), kind=kOutput, calls=%fused_computation.15 | convolution fusion | flops 12885688320 | bytes 56098816 | tf_op jit(solution)/shard_map/td,kdc->ktc/dot_general | solution.py:37
  908.0 1.3 collective-permute-start
  909.3 14.3 %all-gather = f32[64,1024]{1,0:T(8,128)S(1)} all-gather(f32[16,1024]{1,0:T(8,128)S(1)} %get-tuple-element.63), channel_id=2, replica_groups=mesh['seq'=4,'ch'=8] {'seq'}, dimensions={0}, use_global_device_ids=true | all-gather | bytes 327680 | tf_op jit(solution)/shard_map/all_gather | solution.py:17
  923.6 0.6 copy.13
  924.3 0.5 maximum_convert_fusion
  924.7 0.9 fusion.2
  925.7 1.2 fusion.10
  926.8 2.5 copy.12
  929.4 4.1 multiply_reduce_fusion.1
  933.5 14.6 %all-gather.1 = f32[64,1024]{1,0:T(8,128)} all-gather(f32[16,1024]{1,0:T(8,128)S(1)} %multiply_reduce_fusion.1), channel_id=3, replica_groups=mesh['seq'=4,'ch'=8] {'seq'}, dimensions={0}, use_global_device_ids=true | all-gather | bytes 327680 | tf_op jit(solution)/shard_map/all_gather | solution.py:17
  948.1 0.2 while.12
  948.3 0.9 fusion.15
  949.2 3.9 bitcast_multiply_fusion.1
  953.1 0.0 copy-start.2
  953.1 14.0 %multiply_reduce_fusion.2 = f32[256,1024]{1,0:T(8,128)} fusion(f32[16,1024,256]{2,1,0:T(8,128)S(1)} %bitcast.50, f32[16,1024]{1,0:T(8,128)S(1)} %get-tuple-element.61, f32[256]{0:T(256)S(1)} %iota_add_fusion.1, f32[16,1024]{1,0:T(8,128)S(1)} %copy-done.1), kind=kOutput, calls=%fused_computation.5 | convolution fusion | flops 12901482496 | bytes 17957888 | tf_op jit(solution)/shard_map/dot_general | solution.py:67
  967.2 2.8 multiply_reduce_fusion
  970.0 2.6 fusion.12
  (14 shorter events, 0.1 us)
Async XLA Ops:
  6.5 42.0 %all-gather.7.cloned.1.call-start = ((), (), s32[]{:S(2)}) async-start(), calls=%async_computation.1 | async-start | bytes 4718592 | tf_op jit(solution)/shard_map/all_gather | solution.py:36
  7.3 878.9 %all-gather.5.cloned.1.call-start = ((), (), s32[]{:S(2)}) async-start(), calls=%async_computation | async-start | bytes 62914560 | tf_op jit(solution)/shard_map/all_gather | solution.py:40
  10.5 913.1 %copy-start = (f32[16,1024]{1,0:T(8,128)S(1)}, f32[16,1024]{1,0:T(8,128)}, u32[]{:S(2)}) copy-start(f32[16,1024]{1,0:T(8,128)} %param.11) | copy-start | bytes 196612
  908.0 16.3 %collective-permute-start = (bf16[3,2,1024]{2,1,0:T(2,128)(2,1)S(1)}, bf16[3,2,1024]{2,1,0:T(2,128)(2,1)S(1)}, u32[]{:S(2)}, u32[]{:S(2)}) collective-permute-start(bf16[3,2,1024]{2,1,0:T(2,128)(2,1)S(1)} %slice.40), channel_id=1, source_target_pairs={{0,8},{8,16},{16,24},{1,9},{9,17},{17,25},{2,10},{10,18},{18,26},{... | collective-permute-start | bytes 36872 | tf_op jit(solution)/shard_map/ppermute | solution.py:12
  948.3 4.8 copy-start.1
  953.1 16.9 %copy-start.2 = (f32[1024]{0:T(1024)S(1)}, f32[1024]{0:T(1024)}, u32[]{:S(2)}) copy-start(f32[1024]{0:T(1024)} %param.13) | copy-start | bytes 12292
Sparse Core Ops, SparseCore 0:
  9.2 39.2 all-gather.6
  50.1 835.9 all-gather.4
where the time goes:
time: 980 us; the launch traced here: 979 us
  waiting for transfers between devices  877 us (89%)
  matrix products  35.8 us (4%)
  blocking collectives  28.9 us (3%)
  other arithmetic  18.4 us (2%)
  between operations  13.5 us (1%)
    all_gather x1, waiting for transfers between devices, per_device(): lax.all_gather(w_in, 'seq', axis=1, tiled=True)  838 us
    all_gather x1, waiting for transfers between devices, per_device(): features = lax.all_gather(inputs, 'ch', axis=1, tiled=True)  38.1 us
    all_gather x2, blocking collectives, carried_in(): gathered = jax.tree.map(lambda a: lax.all_gather(a, axis), part)  28.9 us
    dot_general x1, matrix products, per_device(): jnp.einsum('td,kdc->ktc', features, lax.all_gather(w_in, 'seq', axis=1, t...  21.8 us
  transfers between devices with their start and end apart: 3, of which 2 were waited for; matrix products, arithmetic and copies ran while one was open for 0% of the time, Pallas kernels for 0%

commit v1 on v0

--- a/solution.py
+++ b/solution.py
@@ -4,6 +4,22 @@
 from jax.sharding import PartitionSpec as P
 
 TAPS = 3
+
+
+def desk_see(patch, mine_x):
+    carry_out, work_now, val = (lax.psum(1, "seq"), lax.axis_index("seq"), patch.shape[1])
+    frames = tuple(((jj, (jj + 1) % carry_out) for jj in range(carry_out)))
+    xs_all = tuple(((jj, (jj - 1) % carry_out) for jj in range(carry_out)))
+    near = carry_out // 2
+    frame_out = part_next = patch
+    mid_arr = mine_x(patch, work_now * val)
+    for num in range(1, near + 1):
+        frame_out = lax.ppermute(frame_out, "seq", frames)
+        if num < carry_out - near:
+            part_next = lax.ppermute(part_next, "seq", perm=xs_all)
+            mid_arr = mid_arr + mine_x(part_next, (work_now + num) % carry_out * val)
+        mid_arr = mid_arr + mine_x(frame_out, (work_now - num) % carry_out * val)
+    return mid_arr
 
 
 def passed_along(block, axis, distance):
@@ -34,11 +50,14 @@
     width = w_in.shape[2]
     modes = rates.shape[0]
     features = lax.all_gather(inputs, "ch", axis=1, tiled=True)
-    proj = jnp.einsum(
-        "td,kdc->ktc",
-        features,
-        lax.all_gather(w_in, "seq", axis=1, tiled=True),
-        preferred_element_type=jnp.float32,
+    proj = desk_see(
+        w_in,
+        lambda own_block, at: jnp.einsum(
+            "td,kdc->ktc",
+            lax.dynamic_slice_in_dim(features, at, own_block.shape[1], axis=1),
+            own_block,
+            preferred_element_type=jnp.float32,
+        ),
     ).astype(jnp.bfloat16)
     prior = passed_along(proj[:, tok_rows - (TAPS - 1) :, :], "seq", 1)
     padded = jnp.concatenate([prior, proj], axis=1).astype(jnp.float32)

time: 980 us -> 901 us (0.919)
  waiting for transfers between devices: 877 us -> 788 us
    all_gather x1 -> x0, waiting for transfers between devices: 838 us -> none  [per_device(): lax.all_gather(w_in, 'seq', axis=1, tiled=True)]
    ppermute x0 -> x3, waiting for transfers between devices: none -> 485 us  [the longest x2 485 us: desk_see(): frame_out = lax.ppermute(frame_out, 'seq', frames)]
    all_gather x1, waiting for transfers between devices: 38.1 us -> 302 us  [per_device(): features = lax.all_gather(inputs, 'ch', axis=1, tiled=True)]
    dot_general x1 -> x4, matrix products: 21.8 us -> 28.1 us  [per_device(): jnp.einsum('td,kdc->ktc', lax.dynamic_slice_in_dim(features, at, own_bloc...]
  transfers between devices with their start and end apart: 3 -> 5, of which waited for: 2 -> 3; matrix products, arithmetic and copies ran while one was open for 0% -> 3% of each run, Pallas kernels for 0% -> 0%
where the time goes in v1:
time: 901 us; the launch traced here: 900 us
  waiting for transfers between devices  788 us (87%)
  matrix products  42 us (5%)
  blocking collectives  28.5 us (3%)
  other arithmetic  17.1 us (2%)
  between operations  13.6 us (2%)
    ppermute x2, waiting for transfers between devices, desk_see(): frame_out = lax.ppermute(frame_out, 'seq', frames)  485 us
    all_gather x1, waiting for transfers between devices, per_device(): features = lax.all_gather(inputs, 'ch', axis=1, tiled=True)  302 us
    all_gather x2, blocking collectives, carried_in(): gathered = jax.tree.map(lambda a: lax.all_gather(a, axis), part)  28.5 us
    dot_general x4, matrix products, per_device(): jnp.einsum('td,kdc->ktc', lax.dynamic_slice_in_dim(features, at, own_bloc...  28.1 us
  transfers between devices with their start and end apart: 5, of which 3 were waited for; matrix products, arithmetic and copies ran while one was open for 3% of the time, Pallas kernels for 0%

profile of v1, /device:TPU:0, one launch (start us, length us, event | category | flops | bytes accessed | tf_op | source)
XLA Modules:
  0.0 900.0 jit_solution(4827386025260264607)
XLA Ops:
  6.5 3.1 collective-permute-start.1
  9.6 2.0 collective-permute-start
  11.6 271.5 %collective-permute-done.1 = bf16[3,2048,1024]{2,1,0:T(8,128)(2,1)} collective-permute-done((bf16[3,2048,1024]{2,1,0:T(8,128)(2,1)}, bf16[3,2048,1024]{2,1,0:T(8,128)(2,1)}, u32[]{:S(2)}, u32[]{:S(2)}) %collective-permute-start.1) | collective-permute-done | bytes 12582944 | tf_op jit(solution)/shard_map/ppermute | solution.py:17
  283.3 0.9 fusion.25
  284.3 1.5 fusion.24
  285.7 302.2 %all-gather.4.cloned.1.call-done = bf16[256,8192]{1,0:T(8,128)(2,1)} async-done(((bf16[256,1024]{1,0:T(8,128)(2,1)}), bf16[256,8192]{1,0:T(8,128)(2,1)}) %all-gather.4.cloned.1.call-update) | async-done | bytes 4194320 | tf_op jit(solution)/shard_map/all_gather | solution.py:52
  587.9 6.9 fusion.11
  594.8 6.4 fusion.7
  601.3 6.4 fusion.9
  607.7 213.9 %collective-permute-done.2 = bf16[3,2048,1024]{2,1,0:T(8,128)(2,1)} collective-permute-done((bf16[3,2048,1024]{2,1,0:T(8,128)(2,1)}, bf16[3,2048,1024]{2,1,0:T(8,128)(2,1)}, u32[]{:S(2)}, u32[]{:S(2)}) %collective-permute-start.2) | collective-permute-done | bytes 12582944 | tf_op jit(solution)/shard_map/ppermute | solution.py:17
  821.6 8.3 fusion.2
  830.0 1.6 collective-permute-start.3
  831.6 14.0 %all-gather = f32[64,1024]{1,0:T(8,128)S(1)} all-gather(f32[16,1024]{1,0:T(8,128)S(1)} %get-tuple-element.63), channel_id=2, replica_groups=mesh['seq'=4,'ch'=8] {'seq'}, dimensions={0}, use_global_device_ids=true | all-gather | bytes 327680 | tf_op jit(solution)/shard_map/all_gather | solution.py:33
  845.6 0.6 copy.13
  846.7 0.9 fusion
  847.6 1.2 fusion.3
  848.8 2.5 copy.12
  851.3 4.1 multiply_reduce_fusion.1
  855.4 14.5 %all-gather.1 = f32[64,1024]{1,0:T(8,128)} all-gather(f32[16,1024]{1,0:T(8,128)S(1)} %multiply_reduce_fusion.1), channel_id=3, replica_groups=mesh['seq'=4,'ch'=8] {'seq'}, dimensions={0}, use_global_device_ids=true | all-gather | bytes 327680 | tf_op jit(solution)/shard_map/all_gather | solution.py:33
  870.2 0.9 fusion.23
  871.1 3.9 bitcast_multiply_fusion.1
  875.0 14.0 %multiply_reduce_fusion.2 = f32[256,1024]{1,0:T(8,128)} fusion(f32[16,1024,256]{2,1,0:T(8,128)S(1)} %bitcast.58, f32[16,1024]{1,0:T(8,128)S(1)} %get-tuple-element.61, f32[256]{0:T(256)S(1)} %iota_add_fusion.1, f32[16,1024]{1,0:T(8,128)S(1)} %copy-done.4), kind=kOutput, calls=%fused_computation.5 | convolution fusion | flops 12901482496 | bytes 17957888 | tf_op jit(solution)/shard_map/dot_general | solution.py:86
  889.0 2.8 multiply_reduce_fusion
  891.8 1.4 fusion.5
  (26 shorter events, 0.8 us)
Async XLA Ops:
  6.5 581.4 %all-gather.4.cloned.1.call-start = ((), (), s32[]{:S(2)}) async-start(), calls=%async_computation | async-start | bytes 4718592 | tf_op jit(solution)/shard_map/all_gather | solution.py:52
  6.5 276.6 %collective-permute-start.1 = (bf16[3,2048,1024]{2,1,0:T(8,128)(2,1)}, bf16[3,2048,1024]{2,1,0:T(8,128)(2,1)}, u32[]{:S(2)}, u32[]{:S(2)}) collective-permute-start(bf16[3,2048,1024]{2,1,0:T(8,128)(2,1)} %param.9), channel_id=1, source_target_pairs={{0,8},{8,16},{16,24},{24,0},{1,9},{9,17},{17,25},{25,1},{2,10},{10... | collective-permute-start | bytes 37748744 | tf_op jit(solution)/shard_map/ppermute | solution.py:17
  9.6 591.7 %collective-permute-start = (bf16[3,2048,1024]{2,1,0:T(8,128)(2,1)}, bf16[3,2048,1024]{2,1,0:T(8,128)(2,1)}, u32[]{:S(2)}, u32[]{:S(2)}) collective-permute-start(bf16[3,2048,1024]{2,1,0:T(8,128)(2,1)} %param.9), channel_id=1, source_target_pairs={{0,24},{8,0},{16,8},{24,16},{1,25},{9,1},{17,9},{25,17},{2,26},{10... | collective-permute-start | bytes 37748744 | tf_op jit(solution)/shard_map/ppermute | solution.py:19
  283.2 538.4 %collective-permute-start.2 = (bf16[3,2048,1024]{2,1,0:T(8,128)(2,1)}, bf16[3,2048,1024]{2,1,0:T(8,128)(2,1)}, u32[]{:S(2)}, u32[]{:S(2)}) collective-permute-start(bf16[3,2048,1024]{2,1,0:T(8,128)(2,1)} %collective-permute-done.1), channel_id=1, source_target_pairs={{0,8},{8,16},{16,24},{24,0},{1,9},{9,17},{17,25},{25,1},{2,10},{10... | collective-permute-start | bytes 37748744 | tf_op jit(solution)/shard_map/ppermute | solution.py:17
  587.9 6.9 copy-start
  607.7 237.9 %copy-start.2 = (f32[16,1024]{1,0:T(8,128)S(1)}, f32[16,1024]{1,0:T(8,128)}, u32[]{:S(2)}) copy-start(f32[16,1024]{1,0:T(8,128)} %param.11) | copy-start | bytes 196612
  830.0 16.3 %collective-permute-start.3 = (bf16[3,2,1024]{2,1,0:T(2,128)(2,1)S(1)}, bf16[3,2,1024]{2,1,0:T(2,128)(2,1)S(1)}, u32[]{:S(2)}, u32[]{:S(2)}) collective-permute-start(bf16[3,2,1024]{2,1,0:T(2,128)(2,1)S(1)} %slice.40), channel_id=1, source_target_pairs={{0,8},{8,16},{16,24},{1,9},{9,17},{17,25},{2,10},{10,18},{18,26},{... | collective-permute-start | bytes 36872 | tf_op jit(solution)/shard_map/ppermute | solution.py:28
  847.6 3.7 copy-start.3
  871.1 3.9 copy-start.4
  889.0 2.8 copy-start.1
  889.0 2.8 copy-start.5
Sparse Core Ops, SparseCore 0:
  283.3 304.5 all-gather.3
